TPU v7x, 128 devices: a whole 4x4x4 slice. The times are simulated.
128 devices in a mesh: guid: 2 (over x_hi), req: 4 (over x_lo, core), seq: 16 (over y, z).
Axes of the slice: x: 4 (x_hi: 2, x_lo: 2; x = x_hi * 2 + x_lo), y: 4, z: 4, core: 2. Of those that a mesh axis runs over, the one named last changes fastest.
Arguments:
- img_hidden: bfloat16 [2, 24, 1024, 1536], P('guid', 'req', 'seq'), may hold values from -6 to 6
- txt_hidden: bfloat16 [2, 24, 192, 1536], P('guid', 'req', 'seq'), may hold values from -6 to 6
- img_mod: float32 [2, 24, 5, 1536], P('guid', 'req')
- txt_mod: float32 [2, 24, 2, 1536], P('guid', 'req'), may hold values from -3 to 3
- w_img_qkv: bfloat16 [1536, 3072], P(('guid', 'req', 'seq')), may hold values from -0.15625 to 0.15625
- w_txt_qkv: bfloat16 [1536, 3072], P(('guid', 'req', 'seq')), may hold values from -0.15625 to 0.15625
- w_out: bfloat16 [1024, 1536], P(('guid', 'req', 'seq')), may hold values from -0.1875 to 0.1875
- w_head: bfloat16 [1536, 64], P(('guid', 'req', 'seq')), may hold values from -0.15625 to 0.15625
- text_lengths: int32 [2, 24], P('guid', 'req'), may hold values from 1 to 154, as said below
- latent: float32 [24, 1024, 64], P('req', 'seq', 'guid'), may hold values from -6 to 6
- step: int32 [1], replicated, may hold values from 0 to 27
Outputs:
- advanced: float32 [24, 1024, 64], P('req', 'seq', 'guid')
- guided: float32 [24, 1024, 64], P('req', 'seq', 'guid')
Inputs may be any that keep to these rules, and one draw needn't show every extreme that they name: `text_lengths`: in each half one prompt has 154 text tokens and another has 1.
All inputs are finite; a program needn't handle non-finite values.
Results may differ from a plain program's by a relative error of at most 0.012.
The roundings to bfloat16 on the way count: a program that leaves them out, or rounds other values in their place, can miss the bound.
Values may be sent and summed in bfloat16 or wider, within the bound.
No kernel may reach another device: no remote copies, remote signals or barrier semaphores. Data moves between devices by JAX's collectives and lax.ppermute only.
A program may use at most 192 MiB of HBM per device.

v0:
```python
import jax
import jax.numpy as jnp
from jax import lax
from jax.sharding import PartitionSpec as P

HD = 64
STEPS = 28
norm_epsilon = 1e-06
flow_shift = 3.0
guide_scale = 4.5


def partner(value, axis, bit):
    mask = 2**bit
    pairs = [(source, source ^ mask) for source in range(lax.axis_size(axis))]
    return lax.ppermute(value, axis, pairs)


def modulate(values_in, shift_vec, scale_vec):
    values_in = values_in.astype(jnp.float32)
    average = jnp.mean(values_in, axis=-1, keepdims=True)
    variance = jnp.mean((values_in - average) ** 2, axis=-1, keepdims=True)
    normed = (values_in - average) * lax.rsqrt(variance + norm_epsilon)
    return (normed * (1.0 + scale_vec[..., None, :]) + shift_vec[..., None, :]).astype(jnp.bfloat16)


def sigma_level(step_value):
    remaining = 1.0 - step_value / STEPS
    return flow_shift * remaining / (1.0 + (flow_shift - 1.0) * remaining)


def local(
    img_hidden,
    txt_hidden,
    img_mod,
    txt_mod,
    w_img_qkv,
    w_txt_qkv,
    w_out,
    w_head,
    text_lengths,
    latent,
    step,
):
    prompts = img_hidden.shape[1]
    img_rows = img_hidden.shape[2]
    txt_rows = txt_hidden.shape[2]
    dev_rows = img_rows + txt_rows
    model_width = img_hidden.shape[3]
    image_in = modulate(img_hidden[0], img_mod[0, :, 0], img_mod[0, :, 1])
    text_in = modulate(txt_hidden[0], txt_mod[0, :, 0], txt_mod[0, :, 1])
    full_img, full_txt, full_head = (
        lax.all_gather(w_img_qkv, ("guid", "req", "seq"), axis=0, tiled=True),
        lax.all_gather(w_txt_qkv, ("guid", "req", "seq"), axis=0, tiled=True),
        lax.all_gather(w_head, ("guid", "req", "seq"), axis=0, tiled=True),
    )
    attn_width = full_img.shape[1] // 3
    head_count = attn_width // HD
    qkv_image = jnp.einsum(
        "prd,de->pre", image_in, full_img, preferred_element_type=jnp.float32
    ).astype(jnp.bfloat16)
    qkv_text = jnp.einsum(
        "prd,de->pre", text_in, full_txt, preferred_element_type=jnp.float32
    ).astype(jnp.bfloat16)
    query_rows = qkv_image[..., :attn_width]
    key_rows = jnp.concatenate(
        [qkv_image[..., attn_width : 2 * attn_width], qkv_text[..., attn_width : 2 * attn_width]],
        axis=1,
    )
    value_rows = jnp.concatenate(
        [qkv_image[..., 2 * attn_width :], qkv_text[..., 2 * attn_width :]], axis=1
    )
    lengths = text_lengths[0]
    query_heads = query_rows.reshape(prompts, img_rows, head_count, HD)
    running = jnp.full((prompts, head_count, img_rows), -1e30, jnp.float32)
    key_piece = lax.all_gather(key_rows, "seq", axis=1, tiled=True)
    value_piece = lax.all_gather(value_rows, "seq", axis=1, tiled=True)
    piece_rows = key_piece.shape[1]
    key_heads = key_piece.reshape(prompts, piece_rows, head_count, HD)
    value_heads = value_piece.reshape(prompts, piece_rows, head_count, HD)
    scores = (
        jnp.einsum("pqhd,pkhd->phqk", query_heads, key_heads, preferred_element_type=jnp.float32)
        * 0.125
    )
    position = jnp.arange(piece_rows, dtype=jnp.int32)
    owner_dev = position // dev_rows
    offset = position % dev_rows
    text_pos = owner_dev * txt_rows + offset - img_rows
    allowed = (offset < img_rows)[None, :] | (text_pos[None, :] < lengths[:, None])
    scores = jnp.where(allowed[:, None, None, :], scores, -1e30)
    newest = jnp.maximum(running, jnp.max(scores, axis=-1))
    weights = jnp.exp(scores - newest[..., None])
    totals = jnp.sum(weights, axis=-1)
    accumulated = jnp.einsum(
        "phqk,pkhd->phqd",
        weights.astype(jnp.bfloat16),
        value_heads,
        preferred_element_type=jnp.float32,
    )
    running, totals, accumulated = (newest, totals, accumulated)
    mixture = accumulated / totals[..., None]
    attended = (
        jnp.transpose(mixture, (0, 2, 1, 3))
        .reshape(prompts, img_rows, attn_width)
        .astype(jnp.bfloat16)
    )
    flattened = attended.reshape(prompts * img_rows, attn_width)
    full_out = lax.all_gather(w_out, ("guid", "req", "seq"), axis=0, tiled=True)
    projected = jnp.dot(flattened, full_out, preferred_element_type=jnp.float32)
    residual = img_hidden[0].astype(jnp.float32) + img_mod[0, :, 2][:, None, :] * projected.reshape(
        prompts, img_rows, model_width
    )
    final_in = modulate(residual, img_mod[0, :, 3], img_mod[0, :, 4])
    guid_index = lax.axis_index("guid")
    half_width = latent.shape[2]
    own_start = guid_index * half_width
    other_start = (1 - guid_index) * half_width
    whole_velocity = jnp.einsum(
        "prd,dc->prc", final_in, full_head, preferred_element_type=jnp.float32
    )
    own_velocity = lax.dynamic_slice_in_dim(whole_velocity, own_start, half_width, 2)
    partner_part = lax.dynamic_slice_in_dim(whole_velocity, other_start, half_width, 2)
    other_velocity = partner(partner_part.astype(jnp.bfloat16), "guid", 0).astype(
        partner_part.dtype
    )
    cond_velocity = jnp.where(guid_index == 0, own_velocity, other_velocity)
    free_velocity = jnp.where(guid_index == 0, other_velocity, own_velocity)
    guided = free_velocity + guide_scale * (cond_velocity - free_velocity)
    step_value = step[0].astype(jnp.float32)
    advanced = latent + (sigma_level(step_value + 1.0) - sigma_level(step_value)) * guided
    return (advanced, guided)


def solution(mesh):
    placed = (
        P("guid", "req", "seq", None),
        P("guid", "req", "seq", None),
        P("guid", "req", None, None),
        P("guid", "req", None, None),
        P(("guid", "req", "seq"), None),
        P(("guid", "req", "seq"), None),
        P(("guid", "req", "seq"), None),
        P(("guid", "req", "seq"), None),
        P("guid", "req"),
        P("req", "seq", "guid"),
        P(),
    )
    return jax.shard_map(
        local,
        mesh=mesh,
        in_specs=placed,
        out_specs=(P("req", "seq", "guid"), P("req", "seq", "guid")),
        check_vma=False,
    )
```

profile of v0, /device:TPU:0, one launch (start us, length us, event | category | flops | bytes accessed | tf_op | source)
XLA Modules:
  0.0 542.6 jit_solution(7397176703256413804)
XLA Ops:
  7.2 0.0 copy-start
  7.2 0.0 all-gather.17.cloned.1.call-start
  7.2 0.7 all-gather.17.cloned.1.call-update
  7.9 0.0 all-gather.15.cloned.1.call-start
  8.0 0.7 all-gather.15.cloned.1.call-update
  8.7 0.0 all-gather.11.cloned.1.call-start
  8.7 1.1 convert_reduce_fusion.1
  9.8 1.2 fusion.38
  11.0 1.5 convert_reduce_fusion
  12.5 0.4 fusion.21
  13.0 0.1 fusion.69
  13.1 0.6 fusion.68
  13.8 0.0 copy-start.1
  13.8 72.9 %all-gather.17.cloned.1.call-done = bf16[128,12,3072]{2,1,0:T(8,128)(2,1)} async-done(((bf16[1,12,3072]{2,1,0:T(8,128)(2,1)}), bf16[128,12,3072]{2,1,0:T(8,128)(2,1)}) %all-gather.17.cloned.1.call-update) | async-done | bytes 9437200 | tf_op jit(solution)/shard_map/all_gather | solution.py:54
  86.7 13.7 %reshape.191 = bf16[1536,3072,1]{1,0,2:T(8,128)(2,1)} reshape(bf16[128,12,3072]{2,1,0:T(8,128)(2,1)} %all-gather.17.cloned.1.call-done) | data formatting | bytes 18874368
  100.3 0.0 copy-done.1
  100.4 5.4 %convolution_convert_fusion.1 = bf16[6,12,3072]{2,1,0:T(8,128)(2,1)S(1)} fusion(bf16[1536,3072,1]{1,0,2:T(8,128)(2,1)} %reshape.191, bf16[1,6,12,1536]{3,2,1,0:T(8,128)(2,1)S(1)} %copy-done.1, f32[6,1536]{1,0:T(8,128)S(1)} %get-tuple-element.20, f32[6,1536]{1,0:T(8,128)S(1)} %get-tuple-element.21, f32[6,12]{1,0:T(8,128)S(1)} %add_rsqrt_fusion.1, ...), kind=kOutput, calls=%fused_computation.11 | convolution fusion | flops 680361984 | bytes 10175040 | tf_op jit(solution)/shard_map/prd,de->pre/dot_general | solution.py:62
  105.8 0.8 fusion.67
  106.6 55.7 %all-gather.15.cloned.1.call-done = bf16[128,12,3072]{2,1,0:T(8,128)(2,1)} async-done(((bf16[1,12,3072]{2,1,0:T(8,128)(2,1)}), bf16[128,12,3072]{2,1,0:T(8,128)(2,1)}) %all-gather.15.cloned.1.call-update) | async-done | bytes 9437200 | tf_op jit(solution)/shard_map/all_gather | solution.py:53
  162.3 13.7 %reshape.190 = bf16[1536,3072,1]{1,0,2:T(8,128)(2,1)} reshape(bf16[128,12,3072]{2,1,0:T(8,128)(2,1)} %all-gather.15.cloned.1.call-done) | data formatting | bytes 18874368
  176.0 7.9 %convolution_convert_fusion = bf16[6,64,3072]{2,1,0:T(8,128)(2,1)S(1)} fusion(bf16[1536,3072,1]{1,0,2:T(8,128)(2,1)} %reshape.190, bf16[1,6,64,1536]{3,2,1,0:T(8,128)(2,1)S(1)} %copy-done, f32[6,1536]{1,0:T(8,128)S(1)} %get-tuple-element.25, f32[6,1536]{1,0:T(8,128)S(1)} %get-tuple-element.24, f32[6,64]{1,0:T(8,128)S(1)} %add_rsqrt_fusion.2, ...), kind=kOutput, calls=%fused_computation.10 | convolution fusion | flops 3628597248 | bytes 13052928 | tf_op jit(solution)/shard_map/prd,de->pre/dot_general | solution.py:59
  183.9 0.2 fusion.66
  184.1 0.7 copy-done.3
  184.8 0.1 pad_maximum_fusion.1
  184.9 1.6 copy.34
  186.5 0.0 all-gather.11.cloned.1.call-update
  186.5 0.0 all-gather.9.cloned.1.call-start
  186.6 0.0 copy-start.8
  186.6 0.0 copy-start.13
  186.6 0.1 pad_maximum_fusion
  186.7 0.0 copy-start.6
  186.7 0.0 copy-start.14
  186.7 1.6 copy.31
  188.3 0.0 all-gather.9.cloned.1.call-update
  188.3 0.0 all-gather.13.cloned.1.call-start
  188.4 0.5 all-gather.13.cloned.1.call-update
  189.0 0.6 copy.65
  189.6 0.0 copy-done.13
  189.6 56.3 %all-gather.2 = bf16[128,12,64]{2,1,0:T(8,128)(2,1)S(1)} all-gather(bf16[1,12,64]{2,1,0:T(8,128)(2,1)S(1)} %bitcast.88), channel_id=1, replica_groups=mesh['guid'=2,'req'=4,'seq'=16] {'guid','req','seq'}, dimensions={0}, use_global_device_ids=true | all-gather | bytes 198144 | tf_op jit(solution)/shard_map/all_gather | solution.py:55
  245.9 0.9 reshape.189
  246.8 0.0 copy-done.6
  246.8 0.6 fusion.51
  247.5 0.1 compare_or_fusion
  247.6 1.0 reshape.170
  248.6 68.5 %all-gather.11.cloned.1.call-done = bf16[6,1216,1024]{2,0,1:T(8,128)(2,1)} async-done(((bf16[6,76,1024]{2,0,1:T(8,128)(2,1)}), bf16[6,1216,1024]{2,0,1:T(8,128)(2,1)}) %all-gather.11.cloned.1.call-update) | async-done | bytes 14942224 | tf_op jit(solution)/shard_map/all_gather | solution.py:77
  317.1 27.3 %copy.35 = bf16[6,1216,1024]{1,2,0:T(8,128)(2,1)} copy(bf16[6,1216,1024]{2,0,1:T(8,128)(2,1)} %all-gather.11.cloned.1.call-done) | data formatting | bytes 29884416 | tf_op jit(solution)/shard_map/all_gather | solution.py:77
  344.4 100.9 %all-gather.9.cloned.1.call-done = bf16[6,1216,1024]{2,0,1:T(8,128)(2,1)} async-done(((bf16[6,76,1024]{2,0,1:T(8,128)(2,1)}), bf16[6,1216,1024]{2,0,1:T(8,128)(2,1)}) %all-gather.9.cloned.1.call-update) | async-done | bytes 14942224 | tf_op jit(solution)/shard_map/all_gather | solution.py:76
  445.3 26.9 %copy.32 = bf16[6,1216,1024]{1,2,0:T(8,128)(2,1)} copy(bf16[6,1216,1024]{2,0,1:T(8,128)(2,1)} %all-gather.9.cloned.1.call-done) | data formatting | bytes 29884416 | tf_op jit(solution)/shard_map/all_gather | solution.py:76
  472.2 15.9 %fusion = (f32[6,16,64]{2,1,0:T(8,128)S(1)}, f32[6,16,64,1216]{3,2,1,0:T(8,128)}) fusion(pred[6,1216]{1,0:T(8,128)(4,1)S(1)} %compare_or_fusion, bf16[6,1216,16,64]{1,3,2,0:T(8,128)(2,1)} %bitcast.82, bf16[6,64,16,64]{3,2,1,0:T(8,128)(2,1)S(1)} %reshape.170), kind=kOutput, calls=%fused_computation.2 | convolution fusion | flops 978708480 | bytes 45644928 | tf_op jit(solution)/shard_map/pqhd,pkhd->phqk/dot_general | solution.py:82
  488.0 14.0 %fusion.1 = f32[6,16,64]{2,1,0:T(8,128)S(1)} fusion(f32[6,16,64,1216]{3,2,1,0:T(8,128)} %get-tuple-element.17, f32[6,16,64]{2,1,0:T(8,128)S(1)} %broadcast_maximum_fusion, pred[6,1216]{1,0:T(8,128)(4,1)S(1)} %compare_or_fusion), kind=kLoop, calls=%fused_computation.3 | loop fusion | flops 29878272 | bytes 29940864 | tf_op jit(solution)/shard_map/reduce_sum | solution.py:93
  502.1 18.7 %fusion.11 = bf16[6,64,16,64]{3,1,2,0:T(8,128)(2,1)} fusion(bf16[6,1216,16,64]{1,3,2,0:T(8,128)(2,1)} %bitcast.83, f32[6,16,64,1216]{3,2,1,0:T(8,128)} %get-tuple-element.17, f32[6,16,64]{2,1,0:T(8,128)S(1)} %broadcast_maximum_fusion, pred[6,1216]{1,0:T(8,128)(4,1)S(1)} %compare_or_fusion, f32[6,64,16]{1,2,0:T(8,128)S(1)} %bitcast.87), kind=kOutput, calls=%fused_computation.15 | convolution fusion | flops 986972160 | bytes 45669504 | tf_op jit(solution)/shard_map/phqk,pkhd->phqd/dot_general | solution.py:94
  520.8 2.4 copy.36
  523.2 1.1 convert_element_type.60
  524.3 0.0 all-gather.13.cloned.1.call-done
  524.4 3.4 fusion.70
  527.7 0.0 copy-start.4
  527.7 0.0 copy-start.11
  527.8 0.0 copy-start.9
  527.8 0.4 multiply_reduce_fusion
  528.2 0.6 copy-done.4
  528.7 0.9 fusion.34
  529.6 3.0 collective-permute-start
  533.4 1.9 collective-permute-done
  535.3 0.7 multiply_add_fusion
  (28 shorter events, 0.2 us)
Async XLA Ops:
  7.2 5.4 copy-start
  7.2 5.8 %copy-start.10 = (f32[1,6,2,1536]{3,2,1,0:T(2,128)S(1)}, f32[1,6,2,1536]{3,2,1,0:T(2,128)}, u32[]{:S(2)}) copy-start(f32[1,6,2,1536]{3,2,1,0:T(2,128)} %param.14) | copy-start | bytes 221188
  7.2 5.9 %copy-start.5 = (f32[1,6,5,1536]{3,0,2,1:T(1,128)S(1)}, f32[1,6,5,1536]{3,0,2,1:T(1,128)}, u32[]{:S(2)}) copy-start(f32[1,6,5,1536]{3,0,2,1:T(1,128)} %param.13) | copy-start | bytes 552964
  7.2 79.5 %all-gather.17.cloned.1.call-start = ((), (), s32[]{:S(2)}) async-start(), calls=%async_computation.4 | async-start | bytes 12681216 | tf_op jit(solution)/shard_map/all_gather | solution.py:54
  7.9 154.4 %all-gather.15.cloned.1.call-start = ((), (), s32[]{:S(2)}) async-start(), calls=%async_computation.3 | async-start | bytes 12681216 | tf_op jit(solution)/shard_map/all_gather | solution.py:53
  8.7 308.4 %all-gather.11.cloned.1.call-start = ((), (), s32[]{:S(2)}) async-start(), calls=%async_computation.1 | async-start | bytes 21168128 | tf_op jit(solution)/shard_map/all_gather | solution.py:77
  13.8 86.6 %copy-start.1 = (bf16[1,6,12,1536]{3,2,1,0:T(8,128)(2,1)S(1)}, bf16[1,6,12,1536]{3,2,1,0:T(8,128)(2,1)}, u32[]{:S(2)}) copy-start(bf16[1,6,12,1536]{3,2,1,0:T(8,128)(2,1)} %param.12) | copy-start | bytes 663556
  183.9 0.9 copy-start.3
  184.9 1.7 copy-start.2
  186.5 258.8 %all-gather.9.cloned.1.call-start = ((), (), s32[]{:S(2)}) async-start(), calls=%async_computation | async-start | bytes 21168128 | tf_op jit(solution)/shard_map/all_gather | solution.py:76
  186.6 2.4 copy-start.8
  186.6 3.0 copy-start.13
  186.7 60.1 %copy-start.6 = (f32[1,6,1,1536]{3,0,2,1:T(1,128)S(1)}, f32[1,6,1,1536]{3,0,2,1:T(1,128)}, u32[]{:S(2)}) copy-start(f32[1,6,1,1536]{3,0,2,1:T(1,128)} %get-tuple-element.9) | copy-start | bytes 110596
  186.7 60.1 %copy-start.7 = (f32[1,6,1,1536]{3,0,2,1:T(1,128)S(1)}, f32[1,6,1,1536]{3,0,2,1:T(1,128)}, u32[]{:S(2)}) copy-start(f32[1,6,1,1536]{3,0,2,1:T(1,128)} %get-tuple-element.12) | copy-start | bytes 110596
  186.7 60.8 %copy-start.14 = (s32[1,6]{1,0:T(1,128)S(1)}, s32[1,6]{1,0:T(1,128)}, u32[]{:S(2)}) copy-start(s32[1,6]{1,0:T(1,128)} %param.19) | copy-start | bytes 76
  188.3 336.0 %all-gather.13.cloned.1.call-start = ((), (), s32[]{:S(2)}) async-start(), calls=%async_computation.2 | async-start | bytes 3170304 | tf_op jit(solution)/shard_map/all_gather | solution.py:108
  527.7 1.0 copy-start.4
  527.7 1.0 copy-start.11
  527.8 1.0 copy-start.12
  527.8 7.5 %copy-start.9 = (f32[6,64,32]{1,2,0:T(8,128)S(1)}, f32[6,64,32]{1,2,0:T(8,128)}, u32[]{:S(2)}) copy-start(f32[6,64,32]{1,2,0:T(8,128)} %param.20) | copy-start | bytes 147460
  529.6 5.7 %collective-permute-start = (bf16[6,64,32]{1,2,0:T(8,128)(2,1)S(1)}, bf16[6,64,32]{1,2,0:T(8,128)(2,1)S(1)}, u32[]{:S(2)}, u32[]{:S(2)}) collective-permute-start(bf16[6,64,32]{1,2,0:T(8,128)(2,1)S(1)} %dynamic-slice_convert_fusion), channel_id=1, source_target_pairs={{0,64},{64,0},{1,65},{65,1},{2,66},{66,2},{3,67},{67,3},{4,68},{68... | collective-permute-start | bytes 73736 | tf_op jit(solution)/shard_map/ppermute | solution.py:16
Sparse Core Ops, SparseCore 0:
  11.1 75.5 all-gather.16
  89.7 72.5 all-gather.14
  186.6 130.4 all-gather.10
  319.1 126.1 all-gather.8
  448.2 65.3 all-gather.12
where the time goes:
time: 545 us; the launch traced here: 543 us
  waiting for transfers between devices  302 us (55%)
  local copies, waits for them, and re-layouts  93.9 us (17%)
  blocking collectives  56.3 us (10%)
  matrix products  52.2 us (10%)
  other arithmetic  20.3 us (4%)
  between operations  14.9 us (3%)
    all_gather x1, waiting for transfers between devices, local(): key_piece = lax.all_gather(key_rows, 'seq', axis=1, tiled=True)  101 us
    all_gather x1, waiting for transfers between devices, local(): lax.all_gather(w_txt_qkv, ('guid', 'req', 'seq'), axis=0, tiled=True)  72.9 us
    all_gather x1, waiting for transfers between devices, local(): value_piece = lax.all_gather(value_rows, 'seq', axis=1, tiled=True)  68.5 us
    all_gather x1, blocking collectives, local(): lax.all_gather(w_head, ('guid', 'req', 'seq'), axis=0, tiled=True)  56.3 us
    all_gather x1, waiting for transfers between devices, local(): lax.all_gather(w_img_qkv, ('guid', 'req', 'seq'), axis=0, tiled=True)  55.7 us
    unnamed x34, local copies, waits for them, and re-layouts  30.3 us
    all_gather x1, local copies, waits for them, and re-layouts, local(): value_piece = lax.all_gather(value_rows, 'seq', axis=1, tiled=True)  27.3 us
    all_gather x1, local copies, waits for them, and re-layouts, local(): key_piece = lax.all_gather(key_rows, 'seq', axis=1, tiled=True)  26.9 us
  transfers between devices with their start and end apart: 6, of which 5 were waited for; matrix products, arithmetic and copies ran while one was open for 25% of the time, Pallas kernels for 0%

commit v1 on v0

--- a/solution.py
+++ b/solution.py
@@ -74,7 +74,26 @@
     query_heads = query_rows.reshape(prompts, img_rows, head_count, HD)
     running = jnp.full((prompts, head_count, img_rows), -1e30, jnp.float32)
     key_piece = lax.all_gather(key_rows, "seq", axis=1, tiled=True)
-    value_piece = lax.all_gather(value_rows, "seq", axis=1, tiled=True)
+    peers, here, width = (lax.axis_size("seq"), lax.axis_index("seq"), value_rows.shape[1])
+    forward = [(i, (i + 1) % peers) for i in range(peers)]
+    backward = [(i, (i - 1) % peers) for i in range(peers)]
+    whole = jnp.zeros(
+        (*value_rows.shape[:1], peers * width, *value_rows.shape[1 + 1 :]), value_rows.dtype
+    )
+    whole = lax.dynamic_update_slice_in_dim(whole, value_rows, here * width, axis=1)
+    from_left = from_right = value_rows
+    half = peers // 2
+    for step_2 in range(1, half + 1):
+        from_left = lax.ppermute(from_left, "seq", forward)
+        whole = lax.dynamic_update_slice_in_dim(
+            whole, from_left, (here - step_2) % peers * width, axis=1
+        )
+        if step_2 < peers - half:
+            from_right = lax.ppermute(from_right, "seq", backward)
+            whole = lax.dynamic_update_slice_in_dim(
+                whole, from_right, (here + step_2) % peers * width, axis=1
+            )
+    value_piece = whole
     piece_rows = key_piece.shape[1]
     key_heads = key_piece.reshape(prompts, piece_rows, head_count, HD)
     value_heads = value_piece.reshape(prompts, piece_rows, head_count, HD)

time: 545 us -> 940 us (1.72); the launches traced: 543 us -> 923 us
  local copies, waits for them, and re-layouts: 93.9 us -> 375 us
  waiting for transfers between devices: 302 us -> 354 us
  starting transfers between devices: 3.24 us -> 39.1 us
  blocking collectives: 56.3 us -> 67.7 us
    dynamic_update_slice x0 -> x16, local copies, waits for them, and re-layouts: none -> 273 us  [the longest x8 138 us: local(): lax.dynamic_update_slice_in_dim(whole, from_left, (here - step_2) % peers...]
    ppermute x0 -> x15, waiting for transfers between devices: none -> 221 us  [the longest x8 203 us: local(): from_left = lax.ppermute(from_left, 'seq', forward)]
    all_gather x1, waiting for transfers between devices: 101 us -> 0.01 us  [local(): key_piece = lax.all_gather(key_rows, 'seq', axis=1, tiled=True)]
    all_gather x1 -> x0, waiting for transfers between devices: 68.5 us -> none  [local(): value_piece = lax.all_gather(value_rows, 'seq', axis=1, tiled=True)]
    ppermute x0 -> x15, starting transfers between devices: none -> 38.9 us  [the longest x7 37.7 us: local(): from_right = lax.ppermute(from_right, 'seq', backward)]
    ppermute x0 -> x15, local copies, waits for them, and re-layouts: none -> 27.3 us  [the longest x8 14.6 us: local(): from_left = lax.ppermute(from_left, 'seq', forward)]
    all_gather x1 -> x0, local copies, waits for them, and re-layouts: 27.3 us -> none  [local(): value_piece = lax.all_gather(value_rows, 'seq', axis=1, tiled=True)]
    all_gather x1, waiting for transfers between devices: 72.9 us -> 52.9 us  [local(): lax.all_gather(w_txt_qkv, ('guid', 'req', 'seq'), axis=0, tiled=True)]
  transfers between devices with their start and end apart: 6 -> 20, of which waited for: 5 -> 14; matrix products, arithmetic and copies ran while one was open for 25% -> 45% of each run, Pallas kernels for 0% -> 0%
where the time goes in v1:
time: 940 us; the launch traced here: 923 us
  local copies, waits for them, and re-layouts  375 us (40%)
  waiting for transfers between devices  354 us (38%)
  blocking collectives  67.7 us (7%)
  matrix products  51.4 us (5%)
  starting transfers between devices  39.1 us (4%)
  other arithmetic  20.3 us (2%)
  between operations  15.2 us (2%)
    ppermute x8, waiting for transfers between devices, local(): from_left = lax.ppermute(from_left, 'seq', forward)  203 us
    dynamic_update_slice x8, local copies, waits for them, and re-layouts, local(): lax.dynamic_update_slice_in_dim(whole, from_left, (here - step_2) % peers...  138 us
    dynamic_update_slice x7, local copies, waits for them, and re-layouts, local(): lax.dynamic_update_slice_in_dim(whole, from_right, (here + step_2) % peer...  120 us
    all_gather x1, waiting for transfers between devices, local(): lax.all_gather(w_img_qkv, ('guid', 'req', 'seq'), axis=0, tiled=True)  73.5 us
    all_gather x1, blocking collectives, local(): lax.all_gather(w_head, ('guid', 'req', 'seq'), axis=0, tiled=True)  67.7 us
    all_gather x1, waiting for transfers between devices, local(): lax.all_gather(w_txt_qkv, ('guid', 'req', 'seq'), axis=0, tiled=True)  52.9 us
    ppermute x7, starting transfers between devices, local(): from_right = lax.ppermute(from_right, 'seq', backward)  37.7 us
    unnamed x48, local copies, waits for them, and re-layouts  31.5 us
  transfers between devices with their start and end apart: 20, of which 14 were waited for; matrix products, arithmetic and copies ran while one was open for 45% of the time, Pallas kernels for 0%

profile of v1, /device:TPU:0, one launch (start us, length us, event | category | flops | bytes accessed | tf_op | source)
XLA Modules:
  0.0 923.1 jit_solution(9650771829424685429)
XLA Ops:
  13.2 73.5 %all-gather.12.cloned.1.call-done = bf16[128,12,3072]{2,1,0:T(8,128)(2,1)} async-done(((bf16[1,12,3072]{2,1,0:T(8,128)(2,1)}), bf16[128,12,3072]{2,1,0:T(8,128)(2,1)}) %all-gather.12.cloned.1.call-update) | async-done | bytes 9437200 | tf_op jit(solution)/shard_map/all_gather | solution.py:53
  86.7 13.7 %reshape.190 = bf16[1536,3072,1]{1,0,2:T(8,128)(2,1)} reshape(bf16[128,12,3072]{2,1,0:T(8,128)(2,1)} %all-gather.12.cloned.1.call-done) | data formatting | bytes 18874368
  100.3 7.9 convolution_convert_fusion
  109.4 52.9 %all-gather.14.cloned.1.call-done = bf16[128,12,3072]{2,1,0:T(8,128)(2,1)} async-done(((bf16[1,12,3072]{2,1,0:T(8,128)(2,1)}), bf16[128,12,3072]{2,1,0:T(8,128)(2,1)}) %all-gather.14.cloned.1.call-update) | async-done | bytes 9437200 | tf_op jit(solution)/shard_map/all_gather | solution.py:54
  162.3 13.7 %reshape.191 = bf16[1536,3072,1]{1,0,2:T(8,128)(2,1)} reshape(bf16[128,12,3072]{2,1,0:T(8,128)(2,1)} %all-gather.14.cloned.1.call-done) | data formatting | bytes 18874368
  176.0 5.4 convolution_convert_fusion.1
  184.5 4.2 collective-permute-start.1
  188.7 33.5 %collective-permute-done = bf16[6,76,1024]{2,1,0:T(8,128)(2,1)S(1)} collective-permute-done((bf16[6,76,1024]{2,1,0:T(8,128)(2,1)S(1)}, bf16[6,76,1024]{2,1,0:T(8,128)(2,1)S(1)}, u32[]{:S(2)}, u32[]{:S(2)}) %collective-permute-start) | collective-permute-done | bytes 933920 | tf_op jit(solution)/shard_map/ppermute | solution.py:87
  222.2 4.4 collective-permute-done.1
  227.6 5.8 collective-permute-start.3
  233.4 18.3 %collective-permute-done.2 = bf16[6,76,1024]{2,1,0:T(8,128)(2,1)S(1)} collective-permute-done((bf16[6,76,1024]{2,1,0:T(8,128)(2,1)S(1)}, bf16[6,76,1024]{2,1,0:T(8,128)(2,1)S(1)}, u32[]{:S(2)}, u32[]{:S(2)}) %collective-permute-start.2) | collective-permute-done | bytes 933920 | tf_op jit(solution)/shard_map/ppermute | solution.py:87
  252.6 4.8 collective-permute-start.5
  257.4 36.6 %collective-permute-done.4 = bf16[6,76,1024]{2,1,0:T(8,128)(2,1)S(1)} collective-permute-done((bf16[6,76,1024]{2,1,0:T(8,128)(2,1)S(1)}, bf16[6,76,1024]{2,1,0:T(8,128)(2,1)S(1)}, u32[]{:S(2)}, u32[]{:S(2)}) %collective-permute-start.4) | collective-permute-done | bytes 933920 | tf_op jit(solution)/shard_map/ppermute | solution.py:87
  294.1 4.5 collective-permute-done.5
  298.6 5.8 collective-permute-start.7
  304.4 36.6 %collective-permute-done.6 = bf16[6,76,1024]{2,1,0:T(8,128)(2,1)S(1)} collective-permute-done((bf16[6,76,1024]{2,1,0:T(8,128)(2,1)S(1)}, bf16[6,76,1024]{2,1,0:T(8,128)(2,1)S(1)}, u32[]{:S(2)}, u32[]{:S(2)}) %collective-permute-start.6) | collective-permute-done | bytes 933920 | tf_op jit(solution)/shard_map/ppermute | solution.py:87
  341.1 4.5 collective-permute-done.7
  345.6 5.8 collective-permute-start.9
  351.4 36.6 %collective-permute-done.8 = bf16[6,76,1024]{2,1,0:T(8,128)(2,1)S(1)} collective-permute-done((bf16[6,76,1024]{2,1,0:T(8,128)(2,1)S(1)}, bf16[6,76,1024]{2,1,0:T(8,128)(2,1)S(1)}, u32[]{:S(2)}, u32[]{:S(2)}) %collective-permute-start.8) | collective-permute-done | bytes 933920 | tf_op jit(solution)/shard_map/ppermute | solution.py:87
  388.1 4.6 collective-permute-done.9
  392.6 5.8 collective-permute-start.11
  398.5 22.6 %collective-permute-done.10 = bf16[6,76,1024]{2,1,0:T(8,128)(2,1)S(1)} collective-permute-done((bf16[6,76,1024]{2,1,0:T(8,128)(2,1)S(1)}, bf16[6,76,1024]{2,1,0:T(8,128)(2,1)S(1)}, u32[]{:S(2)}, u32[]{:S(2)}) %collective-permute-start.10) | collective-permute-done | bytes 933920 | tf_op jit(solution)/shard_map/ppermute | solution.py:87
  421.1 5.4 collective-permute-start.13
  426.5 19.2 %collective-permute-done.12 = bf16[6,76,1024]{2,1,0:T(8,128)(2,1)} collective-permute-done((bf16[6,76,1024]{2,1,0:T(8,128)(2,1)S(1)}, bf16[6,76,1024]{2,1,0:T(8,128)(2,1)}, u32[]{:S(2)}, u32[]{:S(2)}) %collective-permute-start.12) | collective-permute-done | bytes 933920 | tf_op jit(solution)/shard_map/ppermute | solution.py:87
  445.7 67.7 %all-gather.2 = bf16[128,12,64]{2,1,0:T(8,128)(2,1)S(1)} all-gather(bf16[1,12,64]{2,1,0:T(8,128)(2,1)S(1)} %bitcast.88), channel_id=1, replica_groups=mesh['guid'=2,'req'=4,'seq'=16] {'guid','req','seq'}, dimensions={0}, use_global_device_ids=true | all-gather | bytes 198144 | tf_op jit(solution)/shard_map/all_gather | solution.py:55
  516.6 2.5 reshape.170
  519.1 6.4 broadcast_in_dim.19
  525.5 14.9 %dynamic_update_slice.48 = bf16[6,1216,1024]{1,2,0:T(8,128)(2,1)} dynamic-update-slice(bf16[6,1216,1024]{1,2,0:T(8,128)(2,1)} %broadcast_in_dim.19, bf16[6,76,1024]{1,2,0:T(8,128)(2,1)S(1)} %copy.64, s32[]{:T(128)} %constant.152.clone.1, s32[]{:T(128)S(6)} %select_n.161, s32[]{:T(128)} %constant.152.clone.1) | dynamic-update-slice | bytes 1867780 | tf_op jit(solution)/shard_map/dynamic_update_slice | solution.py:83
  540.5 1.8 copy.65
  542.3 17.2 %dynamic_update_slice.49 = bf16[6,1216,1024]{1,2,0:T(8,128)(2,1)} dynamic-update-slice(bf16[6,1216,1024]{1,2,0:T(8,128)(2,1)} %dynamic_update_slice.48, bf16[6,76,1024]{1,2,0:T(8,128)(2,1)S(1)} %copy.65, s32[]{:T(128)} %constant.152.clone.1, s32[]{:T(128)S(6)} %select_n.163, s32[]{:T(128)} %constant.152.clone.1) | dynamic-update-slice | bytes 1867780 | tf_op jit(solution)/shard_map/dynamic_update_slice | solution.py:88
  559.5 1.8 copy.66
  561.3 17.2 %dynamic_update_slice.50 = bf16[6,1216,1024]{1,2,0:T(8,128)(2,1)} dynamic-update-slice(bf16[6,1216,1024]{1,2,0:T(8,128)(2,1)} %dynamic_update_slice.49, bf16[6,76,1024]{1,2,0:T(8,128)(2,1)S(1)} %copy.66, s32[]{:T(128)} %constant.152.clone.1, s32[]{:T(128)S(6)} %select_n.165, s32[]{:T(128)} %constant.152.clone.1) | dynamic-update-slice | bytes 1867780 | tf_op jit(solution)/shard_map/dynamic_update_slice | solution.py:93
  578.5 1.8 copy.67
  580.3 17.2 %dynamic_update_slice.51 = bf16[6,1216,1024]{1,2,0:T(8,128)(2,1)} dynamic-update-slice(bf16[6,1216,1024]{1,2,0:T(8,128)(2,1)} %dynamic_update_slice.50, bf16[6,76,1024]{1,2,0:T(8,128)(2,1)S(1)} %copy.67, s32[]{:T(128)} %constant.152.clone.1, s32[]{:T(128)S(6)} %select_n.167, s32[]{:T(128)} %constant.152.clone.1) | dynamic-update-slice | bytes 1867780 | tf_op jit(solution)/shard_map/dynamic_update_slice | solution.py:88
  597.5 1.8 copy.68
  599.4 17.2 %dynamic_update_slice.52 = bf16[6,1216,1024]{1,2,0:T(8,128)(2,1)} dynamic-update-slice(bf16[6,1216,1024]{1,2,0:T(8,128)(2,1)} %dynamic_update_slice.51, bf16[6,76,1024]{1,2,0:T(8,128)(2,1)S(1)} %copy.68, s32[]{:T(128)} %constant.152.clone.1, s32[]{:T(128)S(6)} %select_n.169, s32[]{:T(128)} %constant.152.clone.1) | dynamic-update-slice | bytes 1867780 | tf_op jit(solution)/shard_map/dynamic_update_slice | solution.py:93
  616.6 1.8 copy.69
  618.4 17.2 %dynamic_update_slice.53 = bf16[6,1216,1024]{1,2,0:T(8,128)(2,1)} dynamic-update-slice(bf16[6,1216,1024]{1,2,0:T(8,128)(2,1)} %dynamic_update_slice.52, bf16[6,76,1024]{1,2,0:T(8,128)(2,1)S(1)} %copy.69, s32[]{:T(128)} %constant.152.clone.1, s32[]{:T(128)S(6)} %select_n.171, s32[]{:T(128)} %constant.152.clone.1) | dynamic-update-slice | bytes 1867780 | tf_op jit(solution)/shard_map/dynamic_update_slice | solution.py:88
  637.5 17.2 %dynamic_update_slice.54 = bf16[6,1216,1024]{1,2,0:T(8,128)(2,1)} dynamic-update-slice(bf16[6,1216,1024]{1,2,0:T(8,128)(2,1)} %dynamic_update_slice.53, bf16[6,76,1024]{1,2,0:T(8,128)(2,1)S(1)} %copy.70, s32[]{:T(128)} %constant.152.clone.1, s32[]{:T(128)S(6)} %select_n.173, s32[]{:T(128)} %constant.152.clone.1) | dynamic-update-slice | bytes 1867780 | tf_op jit(solution)/shard_map/dynamic_update_slice | solution.py:93
  654.7 1.8 copy.71
  656.5 17.2 %dynamic_update_slice.55 = bf16[6,1216,1024]{1,2,0:T(8,128)(2,1)} dynamic-update-slice(bf16[6,1216,1024]{1,2,0:T(8,128)(2,1)} %dynamic_update_slice.54, bf16[6,76,1024]{1,2,0:T(8,128)(2,1)S(1)} %copy.71, s32[]{:T(128)} %constant.152.clone.1, s32[]{:T(128)S(6)} %select_n.175, s32[]{:T(128)} %constant.152.clone.1) | dynamic-update-slice | bytes 1867780 | tf_op jit(solution)/shard_map/dynamic_update_slice | solution.py:88
  673.7 1.8 copy.72
  675.6 17.2 %dynamic_update_slice.56 = bf16[6,1216,1024]{1,2,0:T(8,128)(2,1)} dynamic-update-slice(bf16[6,1216,1024]{1,2,0:T(8,128)(2,1)} %dynamic_update_slice.55, bf16[6,76,1024]{1,2,0:T(8,128)(2,1)S(1)} %copy.72, s32[]{:T(128)} %constant.152.clone.1, s32[]{:T(128)S(6)} %select_n.177, s32[]{:T(128)} %constant.152.clone.1) | dynamic-update-slice | bytes 1867780 | tf_op jit(solution)/shard_map/dynamic_update_slice | solution.py:93
  692.7 1.8 copy.73
  694.6 17.2 %dynamic_update_slice.57 = bf16[6,1216,1024]{1,2,0:T(8,128)(2,1)} dynamic-update-slice(bf16[6,1216,1024]{1,2,0:T(8,128)(2,1)} %dynamic_update_slice.56, bf16[6,76,1024]{1,2,0:T(8,128)(2,1)S(1)} %copy.73, s32[]{:T(128)} %constant.152.clone.1, s32[]{:T(128)S(6)} %select_n.179, s32[]{:T(128)} %constant.152.clone.1) | dynamic-update-slice | bytes 1867780 | tf_op jit(solution)/shard_map/dynamic_update_slice | solution.py:88
  711.8 1.8 copy.74
  713.6 17.2 %dynamic_update_slice.58 = bf16[6,1216,1024]{1,2,0:T(8,128)(2,1)} dynamic-update-slice(bf16[6,1216,1024]{1,2,0:T(8,128)(2,1)} %dynamic_update_slice.57, bf16[6,76,1024]{1,2,0:T(8,128)(2,1)S(1)} %copy.74, s32[]{:T(128)} %constant.152.clone.1, s32[]{:T(128)S(6)} %select_n.181, s32[]{:T(128)} %constant.152.clone.1) | dynamic-update-slice | bytes 1867780 | tf_op jit(solution)/shard_map/dynamic_update_slice | solution.py:93
  730.8 1.8 copy.75
  732.6 17.2 %dynamic_update_slice.59 = bf16[6,1216,1024]{1,2,0:T(8,128)(2,1)} dynamic-update-slice(bf16[6,1216,1024]{1,2,0:T(8,128)(2,1)} %dynamic_update_slice.58, bf16[6,76,1024]{1,2,0:T(8,128)(2,1)S(1)} %copy.75, s32[]{:T(128)} %constant.152.clone.1, s32[]{:T(128)S(6)} %select_n.183, s32[]{:T(128)} %constant.152.clone.1) | dynamic-update-slice | bytes 1867780 | tf_op jit(solution)/shard_map/dynamic_update_slice | solution.py:88
  749.8 1.8 copy.76
  751.6 17.4 %dynamic_update_slice.60 = bf16[6,1216,1024]{1,2,0:T(8,128)(2,1)} dynamic-update-slice(bf16[6,1216,1024]{1,2,0:T(8,128)(2,1)} %dynamic_update_slice.59, bf16[6,76,1024]{1,2,0:T(8,128)(2,1)S(1)} %copy.76, s32[]{:T(128)} %constant.152.clone.1, s32[]{:T(128)S(6)} %select_n.185, s32[]{:T(128)} %constant.152.clone.1) | dynamic-update-slice | bytes 1867780 | tf_op jit(solution)/shard_map/dynamic_update_slice | solution.py:93
  769.0 1.8 copy.77
  770.8 17.2 %dynamic_update_slice.61 = bf16[6,1216,1024]{1,2,0:T(8,128)(2,1)} dynamic-update-slice(bf16[6,1216,1024]{1,2,0:T(8,128)(2,1)} %dynamic_update_slice.60, bf16[6,76,1024]{1,2,0:T(8,128)(2,1)S(1)} %copy.77, s32[]{:T(128)} %constant.152.clone.1, s32[]{:T(128)S(6)} %select_n.187, s32[]{:T(128)} %constant.152.clone.1) | dynamic-update-slice | bytes 1867780 | tf_op jit(solution)/shard_map/dynamic_update_slice | solution.py:88
  788.0 1.8 copy.78
  789.8 17.2 %dynamic_update_slice.62 = bf16[6,1216,1024]{1,2,0:T(8,128)(2,1)} dynamic-update-slice(bf16[6,1216,1024]{1,2,0:T(8,128)(2,1)} %dynamic_update_slice.61, bf16[6,76,1024]{1,2,0:T(8,128)(2,1)S(1)} %copy.78, s32[]{:T(128)} %constant.152.clone.1, s32[]{:T(128)S(6)} %select_n.189, s32[]{:T(128)} %constant.152.clone.1) | dynamic-update-slice | bytes 1867780 | tf_op jit(solution)/shard_map/dynamic_update_slice | solution.py:93
  807.0 1.8 copy.79
  808.9 17.2 %dynamic_update_slice.63 = bf16[6,1216,1024]{1,2,0:T(8,128)(2,1)} dynamic-update-slice(bf16[6,1216,1024]{1,2,0:T(8,128)(2,1)} %dynamic_update_slice.62, bf16[6,76,1024]{1,2,0:T(8,128)(2,1)S(1)} %copy.79, s32[]{:T(128)} %constant.152.clone.1, s32[]{:T(128)S(6)} %select_n.191, s32[]{:T(128)} %constant.152.clone.1) | dynamic-update-slice | bytes 1867780 | tf_op jit(solution)/shard_map/dynamic_update_slice | solution.py:88
  826.0 26.9 %copy.62 = bf16[6,1216,1024]{1,2,0:T(8,128)(2,1)} copy(bf16[6,1216,1024]{2,0,1:T(8,128)(2,1)} %all-gather.8.cloned.1.call-done) | data formatting | bytes 29884416 | tf_op jit(solution)/shard_map/all_gather | solution.py:76
  853.0 15.8 %fusion = (f32[6,16,64]{2,1,0:T(8,128)S(1)}, f32[6,16,64,1216]{3,2,1,0:T(8,128)}) fusion(pred[6,1216]{1,0:T(8,128)(4,1)S(1)} %compare_or_fusion, bf16[6,1216,16,64]{1,3,2,0:T(8,128)(2,1)} %bitcast.82, bf16[6,64,16,64]{3,2,1,0:T(8,128)(2,1)S(1)} %reshape.170), kind=kOutput, calls=%fused_computation.2 | convolution fusion | flops 978708480 | bytes 45644928 | tf_op jit(solution)/shard_map/pqhd,pkhd->phqk/dot_general | solution.py:101
  868.7 14.0 %fusion.1 = f32[6,16,64]{2,1,0:T(8,128)S(1)} fusion(f32[6,16,64,1216]{3,2,1,0:T(8,128)} %get-tuple-element.17, f32[6,16,64]{2,1,0:T(8,128)S(1)} %broadcast_maximum_fusion, pred[6,1216]{1,0:T(8,128)(4,1)S(1)} %compare_or_fusion), kind=kLoop, calls=%fused_computation.3 | loop fusion | flops 29878272 | bytes 29940864 | tf_op jit(solution)/shard_map/reduce_sum | solution.py:112
  882.8 18.0 %fusion.11 = bf16[6,64,16,64]{3,1,2,0:T(8,128)(2,1)} fusion(bf16[6,1216,16,64]{1,3,2,0:T(8,128)(2,1)} %bitcast.83, f32[6,16,64,1216]{3,2,1,0:T(8,128)} %get-tuple-element.17, f32[6,16,64]{2,1,0:T(8,128)S(1)} %broadcast_maximum_fusion, pred[6,1216]{1,0:T(8,128)(4,1)S(1)} %compare_or_fusion, f32[6,64,16]{1,2,0:T(8,128)S(1)} %bitcast.87), kind=kOutput, calls=%fused_computation.15 | convolution fusion | flops 986972160 | bytes 45669504 | tf_op jit(solution)/shard_map/phqk,pkhd->phqd/dot_general | solution.py:113
  900.8 2.5 copy.80
  904.7 3.4 fusion.70
  910.8 4.8 collective-permute-done.15
  (100 shorter events, 21.0 us)
Async XLA Ops:
  7.2 5.4 copy-start
  7.2 5.8 copy-start.17
  7.2 5.9 copy-start.15
  7.2 79.5 %all-gather.12.cloned.1.call-start = ((), (), s32[]{:S(2)}) async-start(), calls=%async_computation.2 | async-start | bytes 12681216 | tf_op jit(solution)/shard_map/all_gather | solution.py:53
  7.9 154.4 %all-gather.14.cloned.1.call-start = ((), (), s32[]{:S(2)}) async-start(), calls=%async_computation.3 | async-start | bytes 12681216 | tf_op jit(solution)/shard_map/all_gather | solution.py:54
  8.7 817.3 %all-gather.8.cloned.1.call-start = ((), (), s32[]{:S(2)}) async-start(), calls=%async_computation | async-start | bytes 21168128 | tf_op jit(solution)/shard_map/all_gather | solution.py:76
  109.4 66.6 %copy-start.2 = (bf16[1,6,12,1536]{3,2,1,0:T(8,128)(2,1)S(1)}, bf16[1,6,12,1536]{3,2,1,0:T(8,128)(2,1)}, u32[]{:S(2)}) copy-start(bf16[1,6,12,1536]{3,2,1,0:T(8,128)(2,1)} %param.12) | copy-start | bytes 663556
  181.5 264.2 %copy-start.20 = (bf16[12,64]{1,0:T(8,128)(2,1)S(1)}, bf16[12,64]{1,0:T(8,128)(2,1)}, u32[]{:S(2)}) copy-start(bf16[12,64]{1,0:T(8,128)(2,1)} %param.18) | copy-start | bytes 4612
  183.1 331.9 %copy-start.21 = (s32[1,6]{1,0:T(1,128)S(1)}, s32[1,6]{1,0:T(1,128)}, u32[]{:S(2)}) copy-start(s32[1,6]{1,0:T(1,128)} %param.19) | copy-start | bytes 76
  183.2 721.5 %all-gather.10.cloned.1.call-start = ((), (), s32[]{:S(2)}) async-start(), calls=%async_computation.1 | async-start | bytes 3170304 | tf_op jit(solution)/shard_map/all_gather | solution.py:127
  183.3 38.9 %collective-permute-start = (bf16[6,76,1024]{2,1,0:T(8,128)(2,1)S(1)}, bf16[6,76,1024]{2,1,0:T(8,128)(2,1)S(1)}, u32[]{:S(2)}, u32[]{:S(2)}) collective-permute-start(bf16[6,76,1024]{2,1,0:T(8,128)(2,1)S(1)} %pad_maximum_fusion.1), channel_id=1, source_target_pairs={{0,1},{1,2},{2,3},{3,4},{4,5},{5,6},{6,7},{7,8},{8,9},{9,10},{10,1... | collective-permute-start | bytes 2801672 | tf_op jit(solution)/shard_map/ppermute | solution.py:87
  184.5 42.1 %collective-permute-start.1 = (bf16[6,76,1024]{2,1,0:T(8,128)(2,1)S(1)}, bf16[6,76,1024]{2,1,0:T(8,128)(2,1)S(1)}, u32[]{:S(2)}, u32[]{:S(2)}) collective-permute-start(bf16[6,76,1024]{2,1,0:T(8,128)(2,1)S(1)} %pad_maximum_fusion.1), channel_id=1, source_target_pairs={{0,15},{1,0},{2,1},{3,2},{4,3},{5,4},{6,5},{7,6},{8,7},{9,8},{10,9... | collective-permute-start | bytes 2801672 | tf_op jit(solution)/shard_map/ppermute | solution.py:92
  222.2 71.8 %copy-start.5 = (bf16[6,76,1024]{2,1,0:T(8,128)(2,1)}, bf16[6,76,1024]{2,1,0:T(8,128)(2,1)S(1)}, u32[]{:S(2)}) copy-start(bf16[6,76,1024]{2,1,0:T(8,128)(2,1)S(1)} %collective-permute-done) | copy-start | bytes 2801668
  222.2 29.4 %collective-permute-start.2 = (bf16[6,76,1024]{2,1,0:T(8,128)(2,1)S(1)}, bf16[6,76,1024]{2,1,0:T(8,128)(2,1)S(1)}, u32[]{:S(2)}, u32[]{:S(2)}) collective-permute-start(bf16[6,76,1024]{2,1,0:T(8,128)(2,1)S(1)} %collective-permute-done), channel_id=1, source_target_pairs={{0,1},{1,2},{2,3},{3,4},{4,5},{5,6},{6,7},{7,8},{8,9},{9,10},{10,1... | collective-permute-start | bytes 2801672 | tf_op jit(solution)/shard_map/ppermute | solution.py:87
  226.6 1.0 copy-start.3
  227.6 24.1 %collective-permute-start.3 = (bf16[6,76,1024]{2,1,0:T(8,128)(2,1)S(1)}, bf16[6,76,1024]{2,1,0:T(8,128)(2,1)S(1)}, u32[]{:S(2)}, u32[]{:S(2)}) collective-permute-start(bf16[6,76,1024]{2,1,0:T(8,128)(2,1)S(1)} %collective-permute-done.1), channel_id=1, source_target_pairs={{0,15},{1,0},{2,1},{3,2},{4,3},{5,4},{6,5},{7,6},{8,7},{9,8},{10,9... | collective-permute-start | bytes 2801672 | tf_op jit(solution)/shard_map/ppermute | solution.py:92
  251.7 0.9 copy-start.4
  251.7 42.4 %collective-permute-start.4 = (bf16[6,76,1024]{2,1,0:T(8,128)(2,1)S(1)}, bf16[6,76,1024]{2,1,0:T(8,128)(2,1)S(1)}, u32[]{:S(2)}, u32[]{:S(2)}) collective-permute-start(bf16[6,76,1024]{2,1,0:T(8,128)(2,1)S(1)} %collective-permute-done.2), channel_id=1, source_target_pairs={{0,1},{1,2},{2,3},{3,4},{4,5},{5,6},{6,7},{7,8},{8,9},{9,10},{10,1... | collective-permute-start | bytes 2801672 | tf_op jit(solution)/shard_map/ppermute | solution.py:87
  252.6 41.4 %copy-start.6 = (bf16[6,76,1024]{2,1,0:T(8,128)(2,1)}, bf16[6,76,1024]{2,1,0:T(8,128)(2,1)S(1)}, u32[]{:S(2)}) copy-start(bf16[6,76,1024]{2,1,0:T(8,128)(2,1)S(1)} %collective-permute-done.3) | copy-start | bytes 2801668
  252.6 46.0 %collective-permute-start.5 = (bf16[6,76,1024]{2,1,0:T(8,128)(2,1)S(1)}, bf16[6,76,1024]{2,1,0:T(8,128)(2,1)S(1)}, u32[]{:S(2)}, u32[]{:S(2)}) collective-permute-start(bf16[6,76,1024]{2,1,0:T(8,128)(2,1)S(1)} %collective-permute-done.3), channel_id=1, source_target_pairs={{0,15},{1,0},{2,1},{3,2},{4,3},{5,4},{6,5},{7,6},{8,7},{9,8},{10,9... | collective-permute-start | bytes 2801672 | tf_op jit(solution)/shard_map/ppermute | solution.py:92
  294.1 4.6 copy-start.7
  294.1 47.0 %collective-permute-start.6 = (bf16[6,76,1024]{2,1,0:T(8,128)(2,1)S(1)}, bf16[6,76,1024]{2,1,0:T(8,128)(2,1)S(1)}, u32[]{:S(2)}, u32[]{:S(2)}) collective-permute-start(bf16[6,76,1024]{2,1,0:T(8,128)(2,1)S(1)} %collective-permute-done.4), channel_id=1, source_target_pairs={{0,1},{1,2},{2,3},{3,4},{4,5},{5,6},{6,7},{7,8},{8,9},{9,10},{10,1... | collective-permute-start | bytes 2801672 | tf_op jit(solution)/shard_map/ppermute | solution.py:87
  298.6 42.5 %copy-start.8 = (bf16[6,76,1024]{2,1,0:T(8,128)(2,1)}, bf16[6,76,1024]{2,1,0:T(8,128)(2,1)S(1)}, u32[]{:S(2)}) copy-start(bf16[6,76,1024]{2,1,0:T(8,128)(2,1)S(1)} %collective-permute-done.5) | copy-start | bytes 2801668
  298.6 47.0 %collective-permute-start.7 = (bf16[6,76,1024]{2,1,0:T(8,128)(2,1)S(1)}, bf16[6,76,1024]{2,1,0:T(8,128)(2,1)S(1)}, u32[]{:S(2)}, u32[]{:S(2)}) collective-permute-start(bf16[6,76,1024]{2,1,0:T(8,128)(2,1)S(1)} %collective-permute-done.5), channel_id=1, source_target_pairs={{0,15},{1,0},{2,1},{3,2},{4,3},{5,4},{6,5},{7,6},{8,7},{9,8},{10,9... | collective-permute-start | bytes 2801672 | tf_op jit(solution)/shard_map/ppermute | solution.py:92
  341.1 4.5 copy-start.9
  341.1 47.0 %collective-permute-start.8 = (bf16[6,76,1024]{2,1,0:T(8,128)(2,1)S(1)}, bf16[6,76,1024]{2,1,0:T(8,128)(2,1)S(1)}, u32[]{:S(2)}, u32[]{:S(2)}) collective-permute-start(bf16[6,76,1024]{2,1,0:T(8,128)(2,1)S(1)} %collective-permute-done.6), channel_id=1, source_target_pairs={{0,1},{1,2},{2,3},{3,4},{4,5},{5,6},{6,7},{7,8},{8,9},{9,10},{10,1... | collective-permute-start | bytes 2801672 | tf_op jit(solution)/shard_map/ppermute | solution.py:87
  345.6 42.5 %copy-start.10 = (bf16[6,76,1024]{2,1,0:T(8,128)(2,1)}, bf16[6,76,1024]{2,1,0:T(8,128)(2,1)S(1)}, u32[]{:S(2)}) copy-start(bf16[6,76,1024]{2,1,0:T(8,128)(2,1)S(1)} %collective-permute-done.7) | copy-start | bytes 2801668
  345.6 47.0 %collective-permute-start.9 = (bf16[6,76,1024]{2,1,0:T(8,128)(2,1)S(1)}, bf16[6,76,1024]{2,1,0:T(8,128)(2,1)S(1)}, u32[]{:S(2)}, u32[]{:S(2)}) collective-permute-start(bf16[6,76,1024]{2,1,0:T(8,128)(2,1)S(1)} %collective-permute-done.7), channel_id=1, source_target_pairs={{0,15},{1,0},{2,1},{3,2},{4,3},{5,4},{6,5},{7,6},{8,7},{9,8},{10,9... | collective-permute-start | bytes 2801672 | tf_op jit(solution)/shard_map/ppermute | solution.py:92
  388.1 4.6 copy-start.11
  388.1 33.0 %collective-permute-start.10 = (bf16[6,76,1024]{2,1,0:T(8,128)(2,1)S(1)}, bf16[6,76,1024]{2,1,0:T(8,128)(2,1)S(1)}, u32[]{:S(2)}, u32[]{:S(2)}) collective-permute-start(bf16[6,76,1024]{2,1,0:T(8,128)(2,1)S(1)} %collective-permute-done.8), channel_id=1, source_target_pairs={{0,1},{1,2},{2,3},{3,4},{4,5},{5,6},{6,7},{7,8},{8,9},{9,10},{10,1... | collective-permute-start | bytes 2801672 | tf_op jit(solution)/shard_map/ppermute | solution.py:87
  392.6 53.1 %copy-start.12 = (bf16[6,76,1024]{2,1,0:T(8,128)(2,1)}, bf16[6,76,1024]{2,1,0:T(8,128)(2,1)S(1)}, u32[]{:S(2)}) copy-start(bf16[6,76,1024]{2,1,0:T(8,128)(2,1)S(1)} %collective-permute-done.9) | copy-start | bytes 2801668
  392.6 28.5 %collective-permute-start.11 = (bf16[6,76,1024]{2,1,0:T(8,128)(2,1)S(1)}, bf16[6,76,1024]{2,1,0:T(8,128)(2,1)}, u32[]{:S(2)}, u32[]{:S(2)}) collective-permute-start(bf16[6,76,1024]{2,1,0:T(8,128)(2,1)S(1)} %collective-permute-done.9), channel_id=1, source_target_pairs={{0,15},{1,0},{2,1},{3,2},{4,3},{5,4},{6,5},{7,6},{8,7},{9,8},{10,9... | collective-permute-start | bytes 2801672 | tf_op jit(solution)/shard_map/ppermute | solution.py:92
  421.0 94.0 %copy-start.13 = (bf16[6,76,1024]{2,1,0:T(8,128)(2,1)}, bf16[6,76,1024]{2,1,0:T(8,128)(2,1)S(1)}, u32[]{:S(2)}) copy-start(bf16[6,76,1024]{2,1,0:T(8,128)(2,1)S(1)} %collective-permute-done.10) | copy-start | bytes 2801668
  421.1 24.7 %collective-permute-start.12 = (bf16[6,76,1024]{2,1,0:T(8,128)(2,1)S(1)}, bf16[6,76,1024]{2,1,0:T(8,128)(2,1)}, u32[]{:S(2)}, u32[]{:S(2)}) collective-permute-start(bf16[6,76,1024]{2,1,0:T(8,128)(2,1)S(1)} %collective-permute-done.10), channel_id=1, source_target_pairs={{0,1},{1,2},{2,3},{3,4},{4,5},{5,6},{6,7},{7,8},{8,9},{9,10},{10,1... | collective-permute-start | bytes 2801672 | tf_op jit(solution)/shard_map/ppermute | solution.py:87
  421.1 366.9 %collective-permute-start.13 = (bf16[6,76,1024]{2,1,0:T(8,128)(2,1)}, bf16[6,76,1024]{2,1,0:T(8,128)(2,1)}, u32[]{:S(2)}, u32[]{:S(2)}) collective-permute-start(bf16[6,76,1024]{2,1,0:T(8,128)(2,1)} %collective-permute-done.11), channel_id=1, source_target_pairs={{0,15},{1,0},{2,1},{3,2},{4,3},{5,4},{6,5},{7,6},{8,7},{9,8},{10,9... | collective-permute-start | bytes 2801672 | tf_op jit(solution)/shard_map/ppermute | solution.py:92
  445.7 361.3 %collective-permute-start.14 = (bf16[6,76,1024]{2,1,0:T(8,128)(2,1)}, bf16[6,76,1024]{2,1,0:T(8,128)(2,1)}, u32[]{:S(2)}, u32[]{:S(2)}) collective-permute-start(bf16[6,76,1024]{2,1,0:T(8,128)(2,1)} %collective-permute-done.12), channel_id=1, source_target_pairs={{0,1},{1,2},{2,3},{3,4},{4,5},{5,6},{6,7},{7,8},{8,9},{9,10},{10,1... | collective-permute-start | bytes 2801672 | tf_op jit(solution)/shard_map/ppermute | solution.py:87
  900.8 3.9 copy-start.1
  908.0 1.0 copy-start.14
  908.1 1.0 copy-start.18
  908.1 1.0 copy-start.19
  908.1 7.5 copy-start.16
  910.0 5.7 collective-permute-start.15
Sparse Core Ops, SparseCore 0:
  11.1 75.5 all-gather.11
  89.7 72.5 all-gather.13
  183.3 227.5 all-gather.7
  421.2 81.6 all-gather.9
